TPU v7x, 256 devices: a whole 4x4x8 slice. The times are simulated.
256 devices in a mesh: tok: 32 (over z, x), tp: 8 (over y, core).
Axes of the slice: x: 4, y: 4, z: 8, core: 2. Of those that a mesh axis runs over, the one named last changes fastest.
Arguments:
- tokens: bfloat16 [16384, 8192], P('tok', 'tp'), may hold values from -6 to 6
- frozen_weight: bfloat16 [8192, 2048], P('tp'), may hold values from -0.0625 to 0.0625
- adapter_down_matrices: bfloat16 [256, 8192, 64], P('tok', 'tp'), may hold values from -0.0625 to 0.0625
- adapter_up_matrices: bfloat16 [256, 64, 2048], P('tok', None, 'tp'), may hold values from -0.75 to 0.75
- adapter_per_block: int32 [1024], P('tok'), may hold values from 0 to 255, as said below
- slot_per_adapter: int32 [256], replicated, may hold values from 0 to 255, as said below
- rank_per_adapter: int32 [256], replicated, may hold values from 16 to 64
- output_gradient: bfloat16 [16384, 2048], P('tok', 'tp'), may hold values from -6 to 6
Outputs:
- projected: bfloat16 [16384, 2048], P('tok', 'tp')
- token_gradient: bfloat16 [16384, 8192], P('tok', 'tp')
- grad_down: float32 [256, 8192, 64], P('tok', 'tp')
- grad_up: float32 [256, 64, 2048], P('tok', None, 'tp')
Inputs may be any that keep to these rules, and one draw needn't show every extreme that they name: `adapter_per_block`: block b covers tokens b * 16 to (b + 1) * 16 - 1. Among the blocks of one index of tok, at most 2 have adapters stored on any one index of tok (slots k with k // 8 equal), and one index of tok receives exactly 2 such blocks from every index. A permutation: adapter a is stored in slot slot_per_adapter[a] of adapter_down_matrices and adapter_up_matrices.
All inputs are finite; a program needn't handle non-finite values.
Results may differ from a plain program's by a relative error of at most 0.0033.
Values may be sent and summed in bfloat16 or wider, within the bound.
No kernel may reach another device: no remote copies, remote signals or barrier semaphores. Data moves between devices by JAX's collectives and lax.ppermute only.
A program may use at most 128 MiB of HBM per device.

v0:
```python
import jax
import jax.numpy as jnp
from jax import lax
from jax.sharding import PartitionSpec as P

ALPHA = 32
BLOCK_TOKENS = 16


def route(block_slot, number_adapters, capacity):
    owner_ids = block_slot // number_adapters
    block_ids = jnp.arange(block_slot.shape[-1], dtype=jnp.int32)
    earlier = (owner_ids[..., :, None] == owner_ids[..., None, :]) & (
        block_ids[None, :] < block_ids[:, None]
    )
    position = jnp.sum(earlier.astype(jnp.int32), axis=-1)
    return owner_ids * capacity + position


def per_device(
    tokens,
    frozen_weight,
    adapter_down_matrices,
    adapter_up_matrices,
    adapter_per_block,
    slot_per_adapter,
    rank_per_adapter,
    output_gradient,
):
    tok_count = lax.axis_size("tok")
    me = lax.axis_index("tok")
    token_rows, width_portion = tokens.shape
    column_portion = output_gradient.shape[1]
    block_count = adapter_per_block.shape[0]
    number_adapters, _, rank_ceiling = adapter_down_matrices.shape
    capacity = max(2, 2 * block_count // tok_count)
    slots = tok_count * capacity
    row_total = slots * BLOCK_TOKENS
    lane = width_portion + column_portion
    block_slot = jnp.take(slot_per_adapter, adapter_per_block)
    destination = route(block_slot, number_adapters, capacity)
    slot_ids = jnp.arange(slots, dtype=jnp.int32)
    hit = destination[None, :] == slot_ids[:, None]
    filled = jnp.any(hit, axis=1)
    source_block = jnp.sum(
        jnp.where(hit, jnp.arange(block_count, dtype=jnp.int32)[None, :], 0), axis=1
    )
    packed = jnp.concatenate(
        [
            tokens.reshape(block_count, BLOCK_TOKENS, width_portion),
            output_gradient.reshape(block_count, BLOCK_TOKENS, column_portion),
        ],
        axis=2,
    )
    send = jnp.where(filled[:, None, None], jnp.take(packed, source_block, axis=0), 0)
    arrived = lax.all_to_all(send, "tok", split_axis=0, concat_axis=0, tiled=True)
    all_blocks = lax.all_gather(adapter_per_block, "tok", axis=0, tiled=False)
    all_slot = jnp.take(slot_per_adapter, all_blocks)
    all_dest = route(all_slot, number_adapters, capacity)
    here = (
        all_dest[:, :, None]
        == (me * capacity + jnp.arange(capacity, dtype=jnp.int32))[None, None, :]
    )
    slot_local = jnp.where(here, (all_slot % number_adapters)[:, :, None] + 1, 0).sum(axis=1) - 1
    slot_adapter = slot_local.reshape(slots)
    input_rows = arrived[:, :, :width_portion].reshape(row_total, width_portion)
    grad_rows = arrived[:, :, width_portion:].reshape(row_total, column_portion)
    stored_ids = me * number_adapters + jnp.arange(number_adapters, dtype=jnp.int32)
    stored_match = slot_per_adapter[None, :] == stored_ids[:, None]
    stored_rank = jnp.sum(jnp.where(stored_match, rank_per_adapter[None, :], 0), axis=1)
    stored_scale = jnp.where(
        stored_rank > 0, jnp.float32(ALPHA) / jnp.maximum(stored_rank, 1).astype(jnp.float32), 0.0
    )
    chosen = slot_adapter[:, None] == jnp.arange(number_adapters, dtype=jnp.int32)[None, :]
    chosen_rows = jnp.broadcast_to(
        chosen[:, None, :], (slots, BLOCK_TOKENS, number_adapters)
    ).reshape(row_total, number_adapters)
    chosen_float = chosen_rows.astype(jnp.float32)
    row_rank = jnp.sum(jnp.where(chosen_rows, stored_rank[None, :], 0), axis=1)
    scale_per_row = jnp.sum(chosen_float * stored_scale[None, :], axis=1)
    keep_cols = jnp.arange(rank_ceiling, dtype=jnp.int32)[None, :] < row_rank[:, None]
    reduced_every_row = jnp.einsum(
        "ue,meb->umb", input_rows, adapter_down_matrices, preferred_element_type=jnp.float32
    )
    low_part = jnp.sum(reduced_every_row * chosen_float[:, :, None], axis=1)
    gathered_every_row = jnp.einsum(
        "hs,gbs->hgb", grad_rows, adapter_up_matrices, preferred_element_type=jnp.float32
    )
    pull_part = jnp.sum(gathered_every_row * chosen_float[:, :, None], axis=1)
    both = lax.psum(jnp.concatenate([low_part, pull_part], axis=1), "tp")
    low_sum = both[:, :rank_ceiling]
    pull_sum = both[:, rank_ceiling:]
    reduced_rows = jnp.where(keep_cols, low_sum, 0.0).astype(jnp.bfloat16)
    reduced_gradient = (scale_per_row[:, None] * jnp.where(keep_cols, pull_sum, 0.0)).astype(
        jnp.bfloat16
    )
    chosen_half = chosen_rows.astype(jnp.bfloat16)
    reduced_picked = chosen_half[:, :, None] * reduced_rows[:, None, :]
    gradient_picked = chosen_half[:, :, None] * reduced_gradient[:, None, :]
    adapter_increment = scale_per_row[:, None] * jnp.einsum(
        "hnq,nqs->hs", reduced_picked, adapter_up_matrices, preferred_element_type=jnp.float32
    )
    grad_down = jnp.einsum(
        "rd,rak->adk", input_rows, gradient_picked, preferred_element_type=jnp.float32
    )
    grad_up = stored_scale[:, None, None] * jnp.einsum(
        "rak,rc->akc", reduced_picked, grad_rows, preferred_element_type=jnp.float32
    )
    adapter_output_rows = jnp.einsum(
        "ymf,mcf->yc", gradient_picked, adapter_down_matrices, preferred_element_type=jnp.float32
    )
    back = jnp.concatenate(
        [
            adapter_output_rows.reshape(slots, BLOCK_TOKENS, width_portion),
            adapter_increment.reshape(slots, BLOCK_TOKENS, column_portion),
        ],
        axis=2,
    )
    returned = lax.all_to_all(back, "tok", split_axis=0, concat_axis=0, tiled=True)
    mine = jnp.take(returned, destination, axis=0)
    base_out = lax.psum_scatter(
        lax.dot_general(
            frozen_weight, tokens, (((0,), (1,)), ((), ())), preferred_element_type=jnp.float32
        ),
        "tp",
        scatter_dimension=0,
        tiled=True,
    ).T
    frozen_input_gradient = lax.dot_general(
        lax.all_gather(output_gradient, "tp", axis=1, tiled=True),
        frozen_weight,
        (((1,), (1,)), ((), ())),
        preferred_element_type=jnp.float32,
    )
    projected = (base_out + mine[:, :, width_portion:].reshape(token_rows, column_portion)).astype(
        jnp.bfloat16
    )
    token_gradient = (
        frozen_input_gradient + mine[:, :, :width_portion].reshape(token_rows, width_portion)
    ).astype(jnp.bfloat16)
    return (projected, token_gradient, grad_down, grad_up)


def solution(mesh):
    return jax.shard_map(
        per_device,
        mesh=mesh,
        in_specs=(
            P("tok", "tp"),
            P("tp", None),
            P("tok", "tp", None),
            P("tok", None, "tp"),
            P("tok"),
            P(),
            P(),
            P("tok", "tp"),
        ),
        out_specs=(P("tok", "tp"), P("tok", "tp"), P("tok", "tp", None), P("tok", None, "tp")),
        check_vma=False,
    )
```

profile of v0, /device:TPU:27, one launch (start us, length us, event | category | flops | bytes accessed | tf_op | source)
XLA Modules:
  0.0 338.1 jit_solution(13137650032125103438)
XLA Ops:
  7.2 0.7 compare_select_fusion.4
  7.9 1.4 gather_fusion
  10.4 1.4 pad_maximum_fusion.1
  11.8 2.2 gather_fusion.2
  14.1 3.7 %select_select_fusion = bf16[64,16,1280]{2,1,0:T(8,128)(2,1)} fusion(bf16[64,16,1280]{2,1,0:T(8,128)(2,1)} %gather_fusion.2, pred[64]{0:T(512)(128)(4,1)S(1)} %compare_and_fusion, pred[64]{0:T(512)(128)(4,1)S(1)} %fusion.30), kind=kLoop, calls=%fused_computation.5 | loop fusion | flops 2621440 | bytes 5243008 | tf_op jit(solution)/shard_map/jit(_where)/select_n | solution.py:55
  17.7 11.2 %all-to-all-start = ((bf16[64,16,1280]{2,1,0:T(8,128)(2,1)}), bf16[64,16,1280]{2,1,0:T(8,128)(2,1)}, u32[]{:S(2)}, u32[]{:S(2)}) async-start(bf16[64,16,1280]{2,1,0:T(8,128)(2,1)} %select_select_fusion), calls=%async_computation.1 | async-start | bytes 5242880 | tf_op jit(solution)/shard_map/all_to_all | solution.py:56
  30.5 61.4 %all-reduce = s32[1024]{0:T(1024)S(1)} all-reduce(s32[1024]{0:T(1024)S(1)} %dynamic-update-slice), channel_id=2, replica_groups=mesh['tok'=32,'tp'=8] {'tok'}, use_global_device_ids=true, to_apply=%add | all-reduce | flops 1024 | bytes 8192
  92.1 6.8 %gather_fusion.1 = s32[1024]{0:T(1024)S(1)} fusion(s32[256]{0:T(256)S(1)} %copy-done.1, s32[1024]{0:T(1024)S(1)} %broadcast_clamp_fusion), kind=kCustom, calls=%fused_computation.1 | custom fusion | bytes 12288 | tf_op jit(solution)/shard_map/jit(_take)/gather | solution.py:58
  99.1 0.8 convert_reduce_fusion
  100.6 1.8 slice.32
  102.5 1.3 fusion.37
  104.0 1.1 slice.33
  105.1 0.8 copy-done.3
  106.4 0.8 pad_maximum_fusion.2
  107.3 7.0 %fusion.36 = f32[2048,512]{1,0:T(8,128)} fusion(bf16[1024,2048]{1,0:T(8,128)(2,1)} %param.9, bf16[512,1024]{1,0:T(8,128)(2,1)} %param.8), kind=kOutput, calls=%fused_computation.86 | convolution fusion | flops 2147483648 | bytes 9437184 | tf_op jit(solution)/shard_map/dot_general | solution.py:122
  116.0 57.9 %all-reduce.3.cloned.1.call-done = f32[1024,128]{0,1:T(8,128)} async-done(((f32[1024,128]{0,1:T(8,128)}), f32[1024,128]{0,1:T(8,128)}) %all-reduce.3.cloned.1.call-update) | async-done | bytes 524304 | tf_op jit(solution)/shard_map/psum | solution.py:90
  173.9 1.0 fusion.26
  174.9 1.5 fusion.11
  176.4 1.3 fusion.6
  177.7 2.9 pad_maximum_fusion
  180.6 9.6 %all-to-all-start.1 = ((f32[64,16,1280]{2,1,0:T(8,128)}), f32[64,16,1280]{2,1,0:T(8,128)}, u32[]{:S(2)}, u32[]{:S(2)}) async-start(f32[64,16,1280]{2,1,0:T(8,128)} %pad_maximum_fusion), calls=%async_computation.2 | async-start | bytes 10485760 | tf_op jit(solution)/shard_map/all_to_all | solution.py:119
  191.0 2.3 fusion.14
  193.3 2.6 convolution_bitcast_fusion
  195.9 116.9 %all-to-all-done.1 = f32[64,16,1280]{2,1,0:T(8,128)} async-done(((f32[64,16,1280]{2,1,0:T(8,128)}), f32[64,16,1280]{2,1,0:T(8,128)}, u32[]{:S(2)}, u32[]{:S(2)}) %all-to-all-start.1) | async-done | bytes 5242912 | tf_op jit(solution)/shard_map/all_to_all | solution.py:119
  312.7 4.7 %gather_fusion.3 = f32[32,16,1280]{2,1,0:T(8,128)} fusion(f32[64,16,1280]{2,1,0:T(8,128)} %all-to-all-done.1, s32[1024]{0:T(1024)S(1)} %pad_clamp_fusion), kind=kCustom, calls=%fused_computation.3 | custom fusion | bytes 5243008 | tf_op jit(solution)/shard_map/jit(_take)/gather | solution.py:120
  317.4 2.0 broadcast_select_fusion
  319.4 0.9 slice.36
  320.3 0.8 copy-done.2
  321.1 2.2 copy.21
  323.3 1.3 fusion.17
  324.6 0.8 copy.22
  325.4 6.2 %fusion = bf16[512,1024]{1,0:T(8,128)(2,1)} fusion(f32[32,16,1024]{2,1,0:T(8,128)S(1)} %slice-done, bf16[512,2048]{1,0:T(8,128)(2,1)} %all-gather.3.cloned.1.call-done, bf16[1024,2048]{1,0:T(8,128)(2,1)} %param.9), kind=kOutput, calls=%fused_computation.7 | convolution fusion | flops 2148532224 | bytes 9437184 | tf_op jit(solution)/shard_map/dot_general | solution.py:129
  (71 shorter events, 6.2 us)
Async XLA Ops:
  7.2 95.3 %copy-start = (bf16[8,1024,64]{1,2,0:T(8,128)(2,1)S(1)}, bf16[8,1024,64]{1,2,0:T(8,128)(2,1)}, u32[]{:S(2)}) copy-start(bf16[8,1024,64]{1,2,0:T(8,128)(2,1)} %param.10) | copy-start | bytes 3145732
  17.7 11.3 %copy-start.8 = (u32[256]{0:T(256)S(1)}, u32[256]{0:T(256)}, u32[]{:S(2)}) copy-start(u32[256]{0:T(256)} %constant.123) | copy-start | bytes 3076
  17.7 12.6 %copy-start.7 = (s32[32]{0:T(128)S(1)}, s32[32]{0:T(128)}, u32[]{:S(2)}) copy-start(s32[32]{0:T(128)} %param.12) | copy-start | bytes 388
  17.7 74.4 %copy-start.1 = (s32[256]{0:T(256)S(1)}, s32[256]{0:T(256)}, u32[]{:S(2)}) copy-start(s32[256]{0:T(256)} %param.13) | copy-start | bytes 3076
  17.7 82.9 %all-to-all-start = ((bf16[64,16,1280]{2,1,0:T(8,128)(2,1)}), bf16[64,16,1280]{2,1,0:T(8,128)(2,1)}, u32[]{:S(2)}, u32[]{:S(2)}) async-start(bf16[64,16,1280]{2,1,0:T(8,128)(2,1)} %select_select_fusion), calls=%async_computation.1 | async-start | bytes 5242880 | tf_op jit(solution)/shard_map/all_to_all | solution.py:56
  29.0 144.9 %all-reduce.3.cloned.1.call-start = ((), (), s32[]{:S(2)}) async-start(), calls=%async_computation.4 | async-start | bytes 1048576 | tf_op jit(solution)/shard_map/psum | solution.py:90
  103.7 2.2 copy-start.6
  105.1 0.8 copy-start.3
  107.3 216.0 %reduce-scatter.2.cloned.1.call-start = ((), (), s32[]{:S(2)}) async-start(), calls=%async_computation.3 | async-start | bytes 4718592 | tf_op jit(solution)/shard_map/reduce_scatter | solution.py:121
  114.3 0.7 copy-start.5
  173.9 2.5 copy-start.4
  180.6 132.1 %all-to-all-start.1 = ((f32[64,16,1280]{2,1,0:T(8,128)}), f32[64,16,1280]{2,1,0:T(8,128)}, u32[]{:S(2)}, u32[]{:S(2)}) async-start(f32[64,16,1280]{2,1,0:T(8,128)} %pad_maximum_fusion), calls=%async_computation.2 | async-start | bytes 10485760 | tf_op jit(solution)/shard_map/all_to_all | solution.py:119
  190.2 135.2 %all-gather.3.cloned.1.call-start = ((), (), s32[]{:S(2)}) async-start(), calls=%async_computation.5 | async-start | bytes 2359296 | tf_op jit(solution)/shard_map/all_gather | solution.py:130
  319.4 1.7 copy-start.2
  321.1 4.3 %slice-start = ((f32[32,16,1280]{2,1,0:T(8,128)}), f32[32,16,1024]{2,1,0:T(8,128)S(1)}, s32[]{:S(2)}) async-start(f32[32,16,1280]{2,1,0:T(8,128)} %copy-done.2), calls=%async_computation.6 | async-start | bytes 4194304 | tf_op jit(solution)/shard_map/slice | solution.py:139
Sparse Core Ops, SparseCore 0:
  107.4 66.4 all-reduce.2
  176.4 40.2 reduce-scatter.1
  218.6 29.6 all-gather.2
where the time goes:
time: 339 us; the launch traced here: 338 us
  waiting for transfers between devices  175 us (52%)
  blocking collectives  61.4 us (18%)
  local copies, waits for them, and re-layouts  26.4 us (8%)
  matrix products  22.5 us (7%)
  starting transfers between devices  21.2 us (6%)
  other arithmetic  16.6 us (5%)
  between operations  14.7 us (4%)
    all_to_all x1, waiting for transfers between devices, per_device(): lax.all_to_all(back, 'tok', split_axis=0, concat_axis=0, tiled=True)  117 us
    unnamed x1, blocking collectives  61.4 us
    psum x1, waiting for transfers between devices, per_device(): both = lax.psum(jnp.concatenate([low_part, pull_part], axis=1), 'tp')  57.9 us
    all_to_all x1, starting transfers between devices, per_device(): lax.all_to_all(send, 'tok', split_axis=0, concat_axis=0, tiled=True)  11.2 us
    all_to_all x1, starting transfers between devices, per_device(): lax.all_to_all(back, 'tok', split_axis=0, concat_axis=0, tiled=True)  9.63 us
    dot_general x1, matrix products, per_device(): lax.dot_general(frozen_weight, tokens, (((0,), (1,)), ((), ())), preferre...  6.97 us
    gather x2, local copies, waits for them, and re-layouts, per_device(): all_slot = jnp.take(slot_per_adapter, all_blocks)  6.9 us
  transfers between devices with their start and end apart: 5, of which 2 were waited for; matrix products, arithmetic and copies ran while one was open for 12% of the time, Pallas kernels for 0%

commit v1 on v0

--- a/solution.py
+++ b/solution.py
@@ -87,7 +87,9 @@
         "hs,gbs->hgb", grad_rows, adapter_up_matrices, preferred_element_type=jnp.float32
     )
     pull_part = jnp.sum(gathered_every_row * chosen_float[:, :, None], axis=1)
-    both = lax.psum(jnp.concatenate([low_part, pull_part], axis=1), "tp")
+    both = jnp.sum(
+        lax.all_gather(jnp.concatenate([low_part, pull_part], axis=1), axis_name="tp"), axis=0
+    )
     low_sum = both[:, :rank_ceiling]
     pull_sum = both[:, rank_ceiling:]
     reduced_rows = jnp.where(keep_cols, low_sum, 0.0).astype(jnp.bfloat16)

time: 339 us -> 312 us (0.920)
  waiting for transfers between devices: 175 us -> 142 us
  local copies, waits for them, and re-layouts: 26.4 us -> 31.9 us
    psum x1 -> x0, waiting for transfers between devices: 57.9 us -> none  [per_device(): both = lax.psum(jnp.concatenate([low_part, pull_part], axis=1), 'tp')]
    all_gather x0 -> x1, waiting for transfers between devices: none -> 26 us  [per_device(): lax.all_gather(jnp.concatenate([low_part, pull_part], axis=1), axis_name=...]
    unnamed x22 -> x23, local copies, waits for them, and re-layouts: 3.89 us -> 9.33 us
  transfers between devices with their start and end apart: 5 -> 5, of which waited for: 2 -> 2; matrix products, arithmetic and copies ran while one was open for 12% -> 15% of each run, Pallas kernels for 0% -> 0%
where the time goes in v1:
time: 312 us; the launch traced here: 309 us
  waiting for transfers between devices  142 us (46%)
  blocking collectives  61.4 us (20%)
  local copies, waits for them, and re-layouts  31.9 us (10%)
  matrix products  21.5 us (7%)
  starting transfers between devices  21.4 us (7%)
  other arithmetic  16.5 us (5%)
  between operations  14.7 us (5%)
    all_to_all x1, waiting for transfers between devices, per_device(): lax.all_to_all(back, 'tok', split_axis=0, concat_axis=0, tiled=True)  115 us
    unnamed x1, blocking collectives  61.4 us
    all_gather x1, waiting for transfers between devices, per_device(): lax.all_gather(jnp.concatenate([low_part, pull_part], axis=1), axis_name=...  26 us
    all_to_all x1, starting transfers between devices, per_device(): lax.all_to_all(send, 'tok', split_axis=0, concat_axis=0, tiled=True)  11.2 us
    all_to_all x1, starting transfers between devices, per_device(): lax.all_to_all(back, 'tok', split_axis=0, concat_axis=0, tiled=True)  9.63 us
    unnamed x23, local copies, waits for them, and re-layouts  9.33 us
    dot_general x1, matrix products, per_device(): lax.dot_general(frozen_weight, tokens, (((0,), (1,)), ((), ())), preferre...  6.97 us
    gather x2, local copies, waits for them, and re-layouts, per_device(): all_slot = jnp.take(slot_per_adapter, all_blocks)  6.9 us
  transfers between devices with their start and end apart: 5, of which 2 were waited for; matrix products, arithmetic and copies ran while one was open for 15% of the time, Pallas kernels for 0%

profile of v1, /device:TPU:27, one launch (start us, length us, event | category | flops | bytes accessed | tf_op | source)
XLA Modules:
  0.0 309.3 jit_solution(3348856729839203404)
XLA Ops:
  7.2 0.7 compare_select_fusion.4
  7.9 1.4 gather_fusion
  10.4 1.4 pad_maximum_fusion.1
  11.8 2.2 gather_fusion.2
  14.1 3.7 %select_select_fusion = bf16[64,16,1280]{2,1,0:T(8,128)(2,1)} fusion(bf16[64,16,1280]{2,1,0:T(8,128)(2,1)} %gather_fusion.2, pred[64]{0:T(512)(128)(4,1)S(1)} %compare_and_fusion, pred[64]{0:T(512)(128)(4,1)S(1)} %fusion.30), kind=kLoop, calls=%fused_computation.6 | loop fusion | flops 2621440 | bytes 5243008 | tf_op jit(solution)/shard_map/jit(_where)/select_n | solution.py:55
  17.7 11.2 %all-to-all-start = ((bf16[64,16,1280]{2,1,0:T(8,128)(2,1)}), bf16[64,16,1280]{2,1,0:T(8,128)(2,1)}, u32[]{:S(2)}, u32[]{:S(2)}) async-start(bf16[64,16,1280]{2,1,0:T(8,128)(2,1)} %select_select_fusion), calls=%async_computation.1 | async-start | bytes 5242880 | tf_op jit(solution)/shard_map/all_to_all | solution.py:56
  30.5 61.4 %all-reduce = s32[1024]{0:T(1024)S(1)} all-reduce(s32[1024]{0:T(1024)S(1)} %dynamic-update-slice), channel_id=2, replica_groups=mesh['tok'=32,'tp'=8] {'tok'}, use_global_device_ids=true, to_apply=%add | all-reduce | flops 1024 | bytes 8192
  92.1 6.8 %gather_fusion.1 = s32[1024]{0:T(1024)S(1)} fusion(s32[256]{0:T(256)S(1)} %copy-done.1, s32[1024]{0:T(1024)S(1)} %broadcast_clamp_fusion), kind=kCustom, calls=%fused_computation.1 | custom fusion | bytes 12288 | tf_op jit(solution)/shard_map/jit(_take)/gather | solution.py:58
  99.1 0.8 convert_reduce_fusion
  100.6 1.8 slice.32
  102.5 1.3 fusion.37
  104.0 1.1 slice.33
  105.1 0.8 copy-done.3
  106.4 0.8 pad_maximum_fusion.2
  107.5 7.0 %fusion.36 = f32[2048,512]{1,0:T(8,128)} fusion(bf16[1024,2048]{1,0:T(8,128)(2,1)} %param.9, bf16[512,1024]{1,0:T(8,128)(2,1)} %param.8), kind=kOutput, calls=%fused_computation.87 | convolution fusion | flops 2147483648 | bytes 9437184 | tf_op jit(solution)/shard_map/dot_general | solution.py:124
  116.2 26.0 %all-gather.7.cloned.1.call-done = f32[8192,128]{0,1:T(8,128)} async-done(((f32[1024,128]{0,1:T(8,128)}), f32[8192,128]{0,1:T(8,128)}) %all-gather.7.cloned.1.call-update) | async-done | bytes 4194320 | tf_op jit(solution)/shard_map/all_gather | solution.py:91
  142.1 5.4 %copy.26 = f32[16,8,8,1024]{3,2,1,0:T(8,128)S(1)} copy(f32[16,8,8,1024]{3,1,2,0:T(8,128)} %bitcast.58) | data formatting | bytes 8388608
  147.6 1.0 bitcast_reduce_fusion
  149.2 1.3 fusion.6
  150.5 2.9 pad_maximum_fusion
  153.3 9.6 %all-to-all-start.1 = ((f32[64,16,1280]{2,1,0:T(8,128)}), f32[64,16,1280]{2,1,0:T(8,128)}, u32[]{:S(2)}, u32[]{:S(2)}) async-start(f32[64,16,1280]{2,1,0:T(8,128)} %pad_maximum_fusion), calls=%async_computation.2 | async-start | bytes 10485760 | tf_op jit(solution)/shard_map/all_to_all | solution.py:121
  163.7 2.3 fusion.14
  166.0 2.6 convolution_bitcast_fusion
  168.6 115.4 %all-to-all-done.1 = f32[64,16,1280]{2,1,0:T(8,128)} async-done(((f32[64,16,1280]{2,1,0:T(8,128)}), f32[64,16,1280]{2,1,0:T(8,128)}, u32[]{:S(2)}, u32[]{:S(2)}) %all-to-all-start.1) | async-done | bytes 5242912 | tf_op jit(solution)/shard_map/all_to_all | solution.py:121
  283.9 4.7 %gather_fusion.3 = f32[32,16,1280]{2,1,0:T(8,128)} fusion(f32[64,16,1280]{2,1,0:T(8,128)} %all-to-all-done.1, s32[1024]{0:T(1024)S(1)} %pad_clamp_fusion), kind=kCustom, calls=%fused_computation.3 | custom fusion | bytes 5243008 | tf_op jit(solution)/shard_map/jit(_take)/gather | solution.py:122
  288.7 2.0 broadcast_select_fusion
  290.6 0.9 slice.36
  291.5 0.8 copy-done.2
  292.3 2.2 copy.24
  294.5 1.3 fusion.17
  295.8 0.8 copy.25
  296.6 6.2 %fusion = bf16[512,1024]{1,0:T(8,128)(2,1)} fusion(f32[32,16,1024]{2,1,0:T(8,128)S(1)} %slice-done, bf16[512,2048]{1,0:T(8,128)(2,1)} %all-gather.5.cloned.1.call-done, bf16[1024,2048]{1,0:T(8,128)(2,1)} %param.9), kind=kOutput, calls=%fused_computation.8 | convolution fusion | flops 2148532224 | bytes 9437184 | tf_op jit(solution)/shard_map/dot_general | solution.py:131
  (73 shorter events, 6.9 us)
Async XLA Ops:
  7.2 95.3 %copy-start = (bf16[8,1024,64]{1,2,0:T(8,128)(2,1)S(1)}, bf16[8,1024,64]{1,2,0:T(8,128)(2,1)}, u32[]{:S(2)}) copy-start(bf16[8,1024,64]{1,2,0:T(8,128)(2,1)} %param.10) | copy-start | bytes 3145732
  17.7 11.3 %copy-start.8 = (u32[256]{0:T(256)S(1)}, u32[256]{0:T(256)}, u32[]{:S(2)}) copy-start(u32[256]{0:T(256)} %constant.123) | copy-start | bytes 3076
  17.7 12.6 %copy-start.7 = (s32[32]{0:T(128)S(1)}, s32[32]{0:T(128)}, u32[]{:S(2)}) copy-start(s32[32]{0:T(128)} %param.12) | copy-start | bytes 388
  17.7 74.4 %copy-start.1 = (s32[256]{0:T(256)S(1)}, s32[256]{0:T(256)}, u32[]{:S(2)}) copy-start(s32[256]{0:T(256)} %param.13) | copy-start | bytes 3076
  17.7 82.9 %all-to-all-start = ((bf16[64,16,1280]{2,1,0:T(8,128)(2,1)}), bf16[64,16,1280]{2,1,0:T(8,128)(2,1)}, u32[]{:S(2)}, u32[]{:S(2)}) async-start(bf16[64,16,1280]{2,1,0:T(8,128)(2,1)} %select_select_fusion), calls=%async_computation.1 | async-start | bytes 5242880 | tf_op jit(solution)/shard_map/all_to_all | solution.py:56
  29.0 113.1 %all-gather.7.cloned.1.call-start = ((), (), s32[]{:S(2)}) async-start(), calls=%async_computation.5 | async-start | bytes 4718592 | tf_op jit(solution)/shard_map/all_gather | solution.py:91
  103.7 2.2 copy-start.5
  105.1 0.8 copy-start.3
  107.3 187.2 %reduce-scatter.2.cloned.1.call-start = ((), (), s32[]{:S(2)}) async-start(), calls=%async_computation.3 | async-start | bytes 4718592 | tf_op jit(solution)/shard_map/reduce_scatter | solution.py:123
  114.5 0.7 copy-start.4
  147.5 1.1 copy-start.6
  153.3 130.6 %all-to-all-start.1 = ((f32[64,16,1280]{2,1,0:T(8,128)}), f32[64,16,1280]{2,1,0:T(8,128)}, u32[]{:S(2)}, u32[]{:S(2)}) async-start(f32[64,16,1280]{2,1,0:T(8,128)} %pad_maximum_fusion), calls=%async_computation.2 | async-start | bytes 10485760 | tf_op jit(solution)/shard_map/all_to_all | solution.py:121
  162.9 133.7 %all-gather.5.cloned.1.call-start = ((), (), s32[]{:S(2)}) async-start(), calls=%async_computation.4 | async-start | bytes 2359296 | tf_op jit(solution)/shard_map/all_gather | solution.py:132
  290.6 1.7 copy-start.2
  292.3 4.3 %slice-start = ((f32[32,16,1280]{2,1,0:T(8,128)}), f32[32,16,1024]{2,1,0:T(8,128)S(1)}, s32[]{:S(2)}) async-start(f32[32,16,1280]{2,1,0:T(8,128)} %copy-done.2), calls=%async_computation.6 | async-start | bytes 4194304 | tf_op jit(solution)/shard_map/slice | solution.py:141
Sparse Core Ops, SparseCore 0:
  107.4 34.6 all-gather.6
  144.7 41.0 reduce-scatter.1
  187.6 29.7 all-gather.4
